TPU v7x, 512 devices: a whole 4x8x8 slice. The times are simulated.
512 devices in a mesh: grp: 16 (over z, core), dev: 32 (over x, y).
Axes of the slice: x: 4, y: 8, z: 8, core: 2. Of those that a mesh axis runs over, the one named last changes fastest.
Arguments:
- ssm_input: bfloat16 [4096, 4096], P('grp', 'dev'), may hold values from -6 to 6
- gate_input: bfloat16 [4096, 4096], P('grp', 'dev'), may hold values from -6 to 6
- step_size: float32 [4096, 64], P('grp', 'dev'), may hold values from 6.1035156e-05 to 0.3375
- decay_rate: float32 [64], P('dev'), may hold values from 0.5 to 2
- in_coeff: bfloat16 [4096, 128], P('grp'), may hold values from -6 to 6
- out_coeff: bfloat16 [4096, 128], P('grp'), may hold values from -6 to 6
- skip_gain: float32 [64], P('dev'), may hold values from 0.5 to 3
- norm_gain: float32 [4096], P('dev'), may hold values from 0.5 to 1.5
- out_proj: bfloat16 [4096, 2048], P(None, 'dev'), may hold values from -0.09375 to 0.09375
- residual: bfloat16 [4096, 2048], P(('grp', 'dev')), may hold values from -6 to 6
- ffn_gain: float32 [2048], replicated, may hold values from 0.5 to 1.5
- router: float32 [2048, 16], replicated, may hold values from -0.125 to 0.125
- routes: int32 [4096, 2], P(('grp', 'dev')), may hold values from 0 to 15, all different within a row; in each aligned block of 8 rows (0 to 7, 8 to 15, ...) at most 2 rows name the same one
- gate_weight: bfloat16 [16, 2048, 8192], P('grp', None, 'dev'), may hold values from -0.125 to 0.125
- up_weight: bfloat16 [16, 2048, 8192], P('grp', None, 'dev'), may hold values from -0.125 to 0.125
- down_weight: bfloat16 [16, 8192, 2048], P('grp', 'dev'), may hold values from -0.0625 to 0.0625
Outputs:
- moe_out: bfloat16 [4096, 2048], P(('grp', 'dev'))
Inputs may be any that keep to these rules, and one draw needn't show every extreme that they name: `routes`: each row names two different experts; among the 8 rows of one dispatch block of consecutive tokens no expert is named more than 2 times, a bound that some block reaches.
All inputs are finite; a program needn't handle non-finite values.
Results may differ from a plain program's by a relative error of at most 0.012.
Values may be sent and summed in bfloat16 or wider, within the bound.
No kernel may reach another device: no remote copies, remote signals or barrier semaphores. Data moves between devices by JAX's collectives and lax.ppermute only.
A program may use at most 64 MiB of HBM per device.

v0:
```python
import jax
import jax.numpy as jnp
from jax import lax
from jax.sharding import Mesh
from jax.sharding import PartitionSpec as P

DEV = ("dev_0", "dev_1")
GRP_DEV = ("grp", "dev_0", "dev_1")
EPSILON = 1e-05
HIGHEST_PREC = lax.Precision.HIGHEST


def side_by_side(arrays, axis, dim, along):
    columns = [a.reshape(*a.shape[:along], -1) for a in arrays]
    both = jnp.concatenate(columns, axis=along)
    filled, at, finished = (lax.all_gather(both, axis, axis=dim, tiled=True), 0, [])
    for a, column in zip(arrays, columns):
        piece = filled[..., at : at + column.shape[along]]
        finished.append(piece.reshape(*piece.shape[:along], *a.shape[along:]))
        at += column.shape[along]
    return tuple(finished)


def sent_to_all(shard, axis):
    peers = lax.axis_size(axis)
    return lax.all_to_all(
        jnp.broadcast_to(shard[None], (peers, *shard.shape)), axis, 0, 0, tiled=True
    )


def of_everyone(shard, axis):
    everything = sent_to_all(shard, axis)
    return jnp.sum(everything, axis=0)


def in_order(tiles, dim):
    dims = list(tiles.shape[1:])
    dims[dim] *= tiles.shape[0]
    return jnp.moveaxis(tiles, 0, dim).reshape(dims)


def collect(shard, axis, dim):
    return in_order(sent_to_all(shard, axis), dim)


def sum_by_axis(terms, axes):
    total = terms.astype(jnp.bfloat16)
    for axis in axes:
        total = lax.psum_scatter(total, axis, scatter_dimension=0, tiled=True)
    return total.astype(jnp.float32)


def rms_scale(values, gain_vec):
    return (
        values * lax.rsqrt(jnp.mean(values * values, axis=-1, keepdims=True) + EPSILON) * gain_vec
    )


def slot_tables(routes_block, expert_count, slot_cap):
    blocks, row_total = (routes_block.shape[0], routes_block.shape[1])
    flat_routes = routes_block.reshape(blocks, row_total * 2)
    onehot = (
        flat_routes[:, :, None] == jnp.arange(expert_count, dtype=jnp.int32)[None, None, :]
    ).astype(jnp.int32)
    earlier = jnp.cumsum(onehot, axis=1) - onehot
    slot_rank = jnp.sum(earlier * onehot, axis=2)
    slot_index = (flat_routes * slot_cap + slot_rank).reshape(blocks, row_total, 2)
    placed = (
        slot_index[:, :, :, None]
        == jnp.arange(expert_count * slot_cap, dtype=jnp.int32)[None, None, None, :]
    )
    return placed.astype(jnp.float32)


def shards(
    ssm_input,
    gate_input,
    step_size,
    decay_rate,
    in_coeff,
    out_coeff,
    skip_gain,
    norm_gain,
    out_proj,
    residual,
    ffn_gain,
    router,
    routes,
    gate_weight,
    up_weight,
    down_weight,
):
    tok_rows = ssm_input.shape[0]
    head_count = step_size.shape[1]
    head_width = ssm_input.shape[1] // head_count
    dev_count = lax.axis_size(DEV)
    inner_dim = ssm_input.shape[1] * dev_count
    block_rows = residual.shape[0]
    model_dim = residual.shape[1]
    experts = lax.axis_size("grp")
    slot_cap = max(2, 4 * block_rows // experts)
    group_slots = experts * slot_cap
    inputs_f = ssm_input.astype(jnp.float32).reshape(tok_rows, head_count, head_width)
    in_float = in_coeff.astype(jnp.float32)
    out_float = out_coeff.astype(jnp.float32)
    log_rate = -(step_size * decay_rate[None, :])
    cumulative = jnp.cumsum(log_rate, axis=0)
    causal = (jnp.arange(tok_rows)[:, None] >= jnp.arange(tok_rows)[None, :])[:, :, None]
    spread = cumulative[:, None, :] - cumulative[None, :, :]
    decay_pair = jnp.where(causal, jnp.exp(jnp.where(causal, spread, 0.0)), 0.0)
    scores = jnp.dot(out_coeff, in_coeff.T, preferred_element_type=jnp.float32)
    mixing = decay_pair * scores[:, :, None] * step_size[None, :, :]
    inside = jnp.einsum("tuh,uhp->thp", mixing, inputs_f, precision=HIGHEST_PREC)
    to_end = jnp.exp(cumulative[-1][None, :] - cumulative) * step_size
    own_state = jnp.einsum("uh,uhp,un->hpn", to_end, inputs_f, in_float, precision=HIGHEST_PREC)
    own_log = cumulative[-1]
    group_logs, group_states = tuple(
        (
            part.astype(jnp.float32)
            for part in side_by_side(
                (own_log[None].astype(jnp.bfloat16), own_state[None].astype(jnp.bfloat16)),
                "grp",
                0,
                2,
            )
        )
    )
    group_index = jnp.arange(group_logs.shape[0])
    my_group = lax.axis_index("grp")
    inclusive = jnp.cumsum(group_logs, axis=0)
    exclusive = inclusive - group_logs
    before_me = jnp.sum(jnp.where((group_index == my_group)[:, None], exclusive, 0.0), axis=0)
    earlier_mask = (group_index < my_group)[:, None]
    weighting = jnp.where(
        earlier_mask, jnp.exp(jnp.where(earlier_mask, before_me[None, :] - inclusive, 0.0)), 0.0
    )
    entering = jnp.einsum("gh,ghpn->hpn", weighting, group_states, precision=HIGHEST_PREC)
    carried = jnp.exp(cumulative)[:, :, None] * jnp.einsum(
        "hpn,tn->thp", entering, out_float, precision=HIGHEST_PREC
    )
    ssm_out = inside + carried + skip_gain[None, :, None] * inputs_f
    gated_out = ssm_out.reshape(tok_rows, head_count * head_width) * jax.nn.silu(
        gate_input.astype(jnp.float32)
    )
    squares = of_everyone(jnp.sum(gated_out * gated_out, axis=1), DEV)
    mixed_rows = (
        gated_out * lax.rsqrt(squares[:, None] / inner_dim + EPSILON) * norm_gain[None, :]
    ).astype(jnp.bfloat16)
    projected = jnp.dot(
        collect(mixed_rows, DEV, 1), out_proj, preferred_element_type=jnp.float32
    ).astype(jnp.bfloat16)
    mamba_out = lax.all_to_all(projected, DEV, split_axis=0, concat_axis=1, tiled=True)
    hidden_res = (residual.astype(jnp.float32) + mamba_out.astype(jnp.float32)).astype(jnp.bfloat16)
    hidden_float = hidden_res.astype(jnp.float32)
    normed = rms_scale(hidden_float, ffn_gain).astype(jnp.bfloat16)
    logits = jnp.dot(normed.astype(jnp.float32), router, precision=HIGHEST_PREC)
    expert_ids = jnp.arange(experts, dtype=jnp.int32)[None, :]
    first_logit = jnp.sum(logits * (routes[:, 0:1] == expert_ids).astype(jnp.float32), axis=1)
    second_logit = jnp.sum(logits * (routes[:, 1:2] == expert_ids).astype(jnp.float32), axis=1)
    first_prob = jax.nn.sigmoid(first_logit - second_logit)
    second_prob = 1.0 - first_prob
    placed = slot_tables(routes[None], experts, slot_cap)[0]
    filled = jnp.sum(placed, axis=1)
    outgoing = jnp.dot(
        filled.T.astype(jnp.bfloat16), normed, preferred_element_type=jnp.float32
    ).astype(jnp.bfloat16)
    outgoing = outgoing.reshape(experts, slot_cap, model_dim)
    arrived = lax.all_to_all(outgoing, "grp", split_axis=0, concat_axis=0, tiled=True)
    all_rows = lax.all_gather(arrived, DEV, axis=0, tiled=True).reshape(-1, model_dim)
    gate_act = jnp.dot(all_rows, gate_weight[0], preferred_element_type=jnp.float32)
    up_act = jnp.dot(all_rows, up_weight[0], preferred_element_type=jnp.float32)
    hidden = (jax.nn.silu(gate_act) * up_act).astype(jnp.bfloat16)
    summed = sum_by_axis(jnp.dot(hidden, down_weight[0], preferred_element_type=jnp.float32), DEV)
    returned = lax.all_to_all(
        summed.astype(jnp.bfloat16).reshape(experts, slot_cap, model_dim),
        "grp",
        split_axis=0,
        concat_axis=0,
        tiled=True,
    )
    weights = first_prob[:, None] * placed[:, 0, :] + second_prob[:, None] * placed[:, 1, :]
    contrib = jnp.dot(
        weights,
        returned.reshape(group_slots, model_dim).astype(jnp.float32),
        precision=HIGHEST_PREC,
    )
    return (hidden_float + contrib).astype(jnp.bfloat16)


def solution(mesh):
    torus = Mesh(mesh.devices.reshape(mesh.shape["grp"], 4, 8), ("grp", "dev_0", "dev_1"))
    in_specs = (
        P("grp", DEV),
        P("grp", DEV),
        P("grp", DEV),
        P(DEV),
        P("grp", None),
        P("grp", None),
        P(DEV),
        P(DEV),
        P(None, DEV),
        P(GRP_DEV, None),
        P(),
        P(),
        P(GRP_DEV, None),
        P("grp", None, DEV),
        P("grp", None, DEV),
        P("grp", DEV, None),
    )
    out_specs = P(GRP_DEV, None)
    return jax.shard_map(
        shards, mesh=torus, in_specs=in_specs, out_specs=out_specs, check_vma=False
    )
```

profile of v0, /device:TPU:1, one launch (start us, length us, event | category | flops | bytes accessed | tf_op | source)
XLA Modules:
  0.0 366.3 jit_solution(13563389187455256031)
XLA Ops:
  6.6 0.9 negate_bitcast_fusion
  7.4 0.6 reduce-window.6
  8.1 0.2 slice_reduce_fusion
  8.2 0.2 reduce-window.9
  8.5 0.2 slice_reduce_fusion.1
  8.7 0.9 copy.73
  9.7 0.8 fusion.55
  10.4 1.0 convolution_convert_fusion.2
  11.5 0.1 pad_maximum_fusion
  11.6 26.0 %all_gather.6 = bf16[16,2,8193]{2,1,0:T(2,128)(2,1)S(1)} all-gather(bf16[1,2,8193]{2,1,0:T(2,128)(2,1)S(1)} %pad_maximum_fusion), channel_id=1, replica_groups=mesh['grp'=16,'dev_0'=4,'dev_1'=8] {'grp'}, dimensions={0}, use_global_device_ids=true | all-gather | bytes 557124 | tf_op jit(solution)/shard_map/all_gather | solution.py:16
  37.6 0.7 slice.40
  38.3 0.1 copy.90
  38.5 0.1 select_reduce_fusion.1
  38.8 0.4 reshape.245
  39.2 1.1 fusion.56
  40.3 0.5 fusion.15
  40.8 0.2 fusion.4
  41.1 0.6 fusion.3
  41.8 0.1 multiply_reduce_fusion
  42.0 18.2 %all_to_all.34 = f32[32,1,256]{2,1,0:T(1,128)S(1)} all-to-all(f32[32,1,256]{2,1,0:T(1,128)S(1)} %broadcast_in_dim.80), channel_id=1, replica_groups=mesh['grp'=16,'dev_0'=4,'dev_1'=8] {'dev_0','dev_1'}, dimensions={0} | all-to-all | bytes 65536 | tf_op jit(solution)/shard_map/all_to_all | solution.py:26
  60.3 0.1 multiply_convert_fusion
  60.4 0.1 copy.80
  60.5 1.6 broadcast_in_dim.81
  62.1 4.1 %all-to-all-start.1 = ((bf16[32,256,128]{1,2,0:T(8,128)(2,1)}), bf16[32,256,128]{1,2,0:T(8,128)(2,1)S(1)}, u32[]{:S(2)}, u32[]{:S(2)}) async-start(bf16[32,256,128]{1,2,0:T(8,128)(2,1)} %broadcast_in_dim.81), calls=%async_computation.1 | async-start | bytes 4194304 | tf_op jit(solution)/shard_map/all_to_all | solution.py:26
  66.5 0.2 select_reduce_fusion
  66.9 48.6 %all-to-all-done.1 = bf16[32,256,128]{1,2,0:T(8,128)(2,1)S(1)} async-done(((bf16[32,256,128]{1,2,0:T(8,128)(2,1)}), bf16[32,256,128]{1,2,0:T(8,128)(2,1)S(1)}, u32[]{:S(2)}, u32[]{:S(2)}) %all-to-all-start.1) | async-done | bytes 2097184 | tf_op jit(solution)/shard_map/all_to_all | solution.py:26
  115.5 1.5 convolution_convert_fusion.3
  117.0 0.1 copy.81
  117.1 0.7 reshape.260
  117.9 6.4 %all-to-all-start.2 = ((bf16[32,2,256]{2,1,0:T(2,128)(2,1)}), bf16[32,2,256]{2,1,0:T(2,128)(2,1)S(1)}, u32[]{:S(2)}, u32[]{:S(2)}) async-start(bf16[32,2,256]{2,1,0:T(2,128)(2,1)} %reshape.260), calls=%async_computation.2 | async-start | bytes 65536 | tf_op jit(solution)/shard_map/all_to_all | solution.py:152
  124.4 8.6 %all-to-all-done.2 = bf16[32,2,256]{2,1,0:T(2,128)(2,1)S(1)} async-done(((bf16[32,2,256]{2,1,0:T(2,128)(2,1)}), bf16[32,2,256]{2,1,0:T(2,128)(2,1)S(1)}, u32[]{:S(2)}, u32[]{:S(2)}) %all-to-all-start.2) | async-done | bytes 32800 | tf_op jit(solution)/shard_map/all_to_all | solution.py:152
  133.1 0.1 reshape.261
  133.2 0.1 reshape.253
  133.3 0.1 fusion.34
  133.5 0.2 convolution_convert_fusion.1
  133.7 0.1 reshape.248
  133.8 14.9 %all_to_all.35 = bf16[16,2,2048]{2,1,0:T(2,128)(2,1)} all-to-all(bf16[16,2,2048]{2,1,0:T(2,128)(2,1)S(1)} %reshape.248), channel_id=1, replica_groups=mesh['grp'=16,'dev_0'=4,'dev_1'=8] {'grp'}, dimensions={0} | all-to-all | bytes 262144 | tf_op jit(solution)/shard_map/all_to_all | solution.py:168
  148.8 73.9 %all-gather.2.cloned.1.call-done = bf16[512,2,2048]{2,1,0:T(2,128)(2,1)} async-done(((bf16[16,2,2048]{2,1,0:T(2,128)(2,1)}), bf16[512,2,2048]{2,1,0:T(2,128)(2,1)}) %all-gather.2.cloned.1.call-update) | async-done | bytes 4194320 | tf_op jit(solution)/shard_map/all_gather | solution.py:169
  222.7 7.2 %reshape.249 = bf16[1024,2048]{1,0:T(8,128)(2,1)} reshape(bf16[512,2,2048]{2,1,0:T(2,128)(2,1)} %all-gather.2.cloned.1.call-done) | data formatting | bytes 8388608 | tf_op jit(solution)/shard_map/reshape | solution.py:169
  229.9 4.5 %fusion.8 = f32[1024,256]{1,0:T(8,128)} fusion(bf16[1024,2048]{1,0:T(8,128)(2,1)} %reshape.249, bf16[1,2048,256]{2,1,0:T(8,128)(2,1)S(1)} %copy-done.8), kind=kOutput, calls=%fused_computation.15 | convolution fusion | flops 1073741824 | bytes 6291456 | tf_op jit(solution)/shard_map/dot_general | solution.py:170
  234.4 9.1 %convolution_convert_fusion = bf16[1024,2048]{1,0:T(8,128)(2,1)} fusion(bf16[1024,2048]{1,0:T(8,128)(2,1)} %reshape.249, bf16[1,256,2048]{2,1,0:T(8,128)(2,1)S(1)} %copy-done, bf16[1,2048,256]{2,1,0:T(8,128)(2,1)} %param.30, f32[1024,256]{1,0:T(8,128)} %fusion.8), kind=kOutput, calls=%fused_computation | convolution fusion | flops 2151153664 | bytes 11534336 | tf_op jit(solution)/shard_map/dot_general | solution.py:173
  243.6 52.5 %reduce-scatter.3.cloned.1.call-done = bf16[256,2048]{1,0:T(8,128)(2,1)} async-done(((bf16[1024,2048]{1,0:T(8,128)(2,1)}), bf16[256,2048]{1,0:T(8,128)(2,1)}) %reduce-scatter.3.cloned.1.call-update) | async-done | bytes 1048592 | tf_op jit(solution)/shard_map/reduce_scatter | solution.py:49
  296.2 39.4 %reduce-scatter.5.cloned.1.call-done = bf16[32,2048]{1,0:T(8,128)(2,1)} async-done(((bf16[256,2048]{1,0:T(8,128)(2,1)}), bf16[32,2048]{1,0:T(8,128)(2,1)}) %reduce-scatter.5.cloned.1.call-update) | async-done | bytes 131088 | tf_op jit(solution)/shard_map/reduce_scatter | solution.py:49
  335.6 1.6 reshape.250
  337.2 12.5 %all-to-all-start.4 = ((bf16[16,2,2048]{2,1,0:T(2,128)(2,1)}), bf16[16,2,2048]{2,1,0:T(2,128)(2,1)S(1)}, u32[]{:S(2)}, u32[]{:S(2)}) async-start(bf16[16,2,2048]{2,1,0:T(2,128)(2,1)} %reshape.250), calls=%async_computation.6 | async-start | bytes 262144 | tf_op jit(solution)/shard_map/all_to_all | solution.py:174
  349.7 0.3 select_reduce_fusion.2
  350.1 8.8 %all-to-all-done.4 = bf16[16,2,2048]{2,1,0:T(2,128)(2,1)S(1)} async-done(((bf16[16,2,2048]{2,1,0:T(2,128)(2,1)}), bf16[16,2,2048]{2,1,0:T(2,128)(2,1)S(1)}, u32[]{:S(2)}, u32[]{:S(2)}) %all-to-all-start.4) | async-done | bytes 131104 | tf_op jit(solution)/shard_map/all_to_all | solution.py:174
  358.9 0.9 fusion
  (60 shorter events, 1.6 us)
Async XLA Ops:
  6.5 227.9 %copy-start = (bf16[1,256,2048]{2,1,0:T(8,128)(2,1)S(1)}, bf16[1,256,2048]{2,1,0:T(8,128)(2,1)}, u32[]{:S(2)}) copy-start(bf16[1,256,2048]{2,1,0:T(8,128)(2,1)} %param.31) | copy-start | bytes 3145732
  6.5 34.5 %copy-start.5 = (f32[256,2]{0,1:T(2,128)S(1)}, f32[256,2]{0,1:T(2,128)}, u32[]{:S(2)}) copy-start(f32[256,2]{0,1:T(2,128)} %param.18) | copy-start | bytes 6148
  6.5 34.3 %copy-start.2 = (bf16[256,128]{1,0:T(8,128)(2,1)S(1)}, bf16[256,128]{1,0:T(8,128)(2,1)}, u32[]{:S(2)}) copy-start(bf16[256,128]{1,0:T(8,128)(2,1)} %param.21) | copy-start | bytes 196612
  6.5 34.5 %copy-start.10 = (f32[2]{0:T(128)S(1)}, f32[2]{0:T(128)}, u32[]{:S(2)}) copy-start(f32[2]{0:T(128)} %param.22) | copy-start | bytes 28
  6.5 35.3 %copy-start.1 = (bf16[256,128]{1,0:T(8,128)(2,1)S(1)}, bf16[256,128]{1,0:T(8,128)(2,1)}, u32[]{:S(2)}) copy-start(bf16[256,128]{1,0:T(8,128)(2,1)} %param.17) | copy-start | bytes 196612
  6.5 53.7 %copy-start.7 = (f32[128]{0:T(128)S(1)}, f32[128]{0:T(128)}, u32[]{:S(2)}) copy-start(f32[128]{0:T(128)} %param.23) | copy-start | bytes 1540
  41.1 25.2 %copy-start.6 = (s32[8,2]{0,1:T(2,128)S(1)}, s32[8,2]{0,1:T(2,128)}, u32[]{:S(2)}) copy-start(s32[8,2]{0,1:T(2,128)} %param.28) | copy-start | bytes 196
  62.1 71.2 %copy-start.3 = (bf16[8,2048]{1,0:T(8,128)(2,1)S(1)}, bf16[8,2048]{1,0:T(8,128)(2,1)}, u32[]{:S(2)}) copy-start(bf16[8,2048]{1,0:T(8,128)(2,1)} %param.25) | copy-start | bytes 98308
  62.1 71.4 %copy-start.4 = (f32[2048]{0:T(1024)S(1)}, f32[2048]{0:T(1024)}, u32[]{:S(2)}) copy-start(f32[2048]{0:T(1024)} %param.26) | copy-start | bytes 24580
  62.1 53.4 %all-to-all-start.1 = ((bf16[32,256,128]{1,2,0:T(8,128)(2,1)}), bf16[32,256,128]{1,2,0:T(8,128)(2,1)S(1)}, u32[]{:S(2)}, u32[]{:S(2)}) async-start(bf16[32,256,128]{1,2,0:T(8,128)(2,1)} %broadcast_in_dim.81), calls=%async_computation.1 | async-start | bytes 4194304 | tf_op jit(solution)/shard_map/all_to_all | solution.py:26
  117.9 15.2 %all-to-all-start.2 = ((bf16[32,2,256]{2,1,0:T(2,128)(2,1)}), bf16[32,2,256]{2,1,0:T(2,128)(2,1)S(1)}, u32[]{:S(2)}, u32[]{:S(2)}) async-start(bf16[32,2,256]{2,1,0:T(2,128)(2,1)} %reshape.260), calls=%async_computation.2 | async-start | bytes 65536 | tf_op jit(solution)/shard_map/all_to_all | solution.py:152
  124.3 98.4 %all-gather.2.cloned.1.call-start = ((), (), s32[]{:S(2)}) async-start(), calls=%async_computation.7 | async-start | bytes 4325376 | tf_op jit(solution)/shard_map/all_gather | solution.py:169
  148.8 81.2 %copy-start.8 = (bf16[1,2048,256]{2,1,0:T(8,128)(2,1)S(1)}, bf16[1,2048,256]{2,1,0:T(8,128)(2,1)}, u32[]{:S(2)}) copy-start(bf16[1,2048,256]{2,1,0:T(8,128)(2,1)} %param.29) | copy-start | bytes 3145732
  148.8 147.3 %reduce-scatter.3.cloned.1.call-start = ((), (), s32[]{:S(2)}) async-start(), calls=%async_computation.8 | async-start | bytes 5242880 | tf_op jit(solution)/shard_map/reduce_scatter | solution.py:49
  243.5 106.1 %copy-start.9 = (f32[2048,16]{0,1:T(8,128)S(1)}, f32[2048,16]{0,1:T(8,128)}, u32[]{:S(2)}) copy-start(f32[2048,16]{0,1:T(8,128)} %param.27) | copy-start | bytes 393220
  243.6 92.0 %reduce-scatter.5.cloned.1.call-start = ((), (), s32[]{:S(2)}) async-start(), calls=%async_computation.9 | async-start | bytes 1179648 | tf_op jit(solution)/shard_map/reduce_scatter | solution.py:49
  337.2 21.6 %all-to-all-start.4 = ((bf16[16,2,2048]{2,1,0:T(2,128)(2,1)}), bf16[16,2,2048]{2,1,0:T(2,128)(2,1)S(1)}, u32[]{:S(2)}, u32[]{:S(2)}) async-start(bf16[16,2,2048]{2,1,0:T(2,128)(2,1)} %reshape.250), calls=%async_computation.6 | async-start | bytes 262144 | tf_op jit(solution)/shard_map/all_to_all | solution.py:174
Sparse Core Ops, SparseCore 0:
  148.9 73.7 all-gather.1
  243.7 52.3 reduce-scatter.2
  299.1 36.3 reduce-scatter.4
where the time goes:
time: 367 us; the launch traced here: 366 us
  waiting for transfers between devices  232 us (63%)
  blocking collectives  59.1 us (16%)
  starting transfers between devices  23.1 us (6%)
  matrix products  20.1 us (5%)
  local copies, waits for them, and re-layouts  15 us (4%)
  between operations  13.4 us (4%)
  other arithmetic  3.74 us (1%)
    reduce_scatter x2, waiting for transfers between devices, sum_by_axis(): total = lax.psum_scatter(total, axis, scatter_dimension=0, tiled=True)  91.8 us
    all_gather x1, waiting for transfers between devices, shards(): lax.all_gather(arrived, DEV, axis=0, tiled=True).reshape(-1, model_dim)  73.9 us
    all_to_all x1, waiting for transfers between devices, sent_to_all(): lax.all_to_all(jnp.broadcast_to(shard[None], (peers, *shard.shape)), axis...  48.6 us
    all_gather x1, blocking collectives, side_by_side(): lax.all_gather(both, axis, axis=dim, tiled=True)  26 us
    all_to_all x1, blocking collectives, sent_to_all(): lax.all_to_all(jnp.broadcast_to(shard[None], (peers, *shard.shape)), axis...  18.2 us
    all_to_all x1, blocking collectives, shards(): lax.all_to_all(outgoing, 'grp', split_axis=0, concat_axis=0, tiled=True)  14.9 us
    all_to_all x1, starting transfers between devices, shards(): lax.all_to_all(summed.astype(jnp.bfloat16).reshape(experts, slot_cap, mod...  12.5 us
    dot_general x1, matrix products, shards(): jnp.dot(hidden, down_weight[0], preferred_element_type=jnp.float32)  9.1 us
  transfers between devices with their start and end apart: 6, of which 6 were waited for; matrix products, arithmetic and copies ran while one was open for 0% of the time, Pallas kernels for 0%

commit v1 on v0

--- a/solution.py
+++ b/solution.py
@@ -1,3 +1,4 @@
+import functools
 import jax
 import jax.numpy as jnp
 from jax import lax
@@ -8,6 +9,18 @@
 GRP_DEV = ("grp", "dev_0", "dev_1")
 EPSILON = 1e-05
 HIGHEST_PREC = lax.Precision.HIGHEST
+
+
+def edit_chains(base_x, dev_axis):
+    return jnp.concatenate(
+        lax.all_to_all(
+            jnp.stack([base_x] * lax.axis_size(dev_axis)), dev_axis, split_axis=0, concat_axis=0
+        ),
+        axis=0,
+    )
+
+
+process_desk_now = functools.partial(edit_chains, dev_axis=DEV)
 
 
 def side_by_side(arrays, axis, dim, along):
@@ -166,7 +179,7 @@
     ).astype(jnp.bfloat16)
     outgoing = outgoing.reshape(experts, slot_cap, model_dim)
     arrived = lax.all_to_all(outgoing, "grp", split_axis=0, concat_axis=0, tiled=True)
-    all_rows = lax.all_gather(arrived, DEV, axis=0, tiled=True).reshape(-1, model_dim)
+    all_rows = process_desk_now(arrived).reshape(-1, model_dim)
     gate_act = jnp.dot(all_rows, gate_weight[0], preferred_element_type=jnp.float32)
     up_act = jnp.dot(all_rows, up_weight[0], preferred_element_type=jnp.float32)
     hidden = (jax.nn.silu(gate_act) * up_act).astype(jnp.bfloat16)

time: 367 us -> 388 us (1.057)
  blocking collectives: 59.1 us -> 157 us
  waiting for transfers between devices: 232 us -> 151 us
  local copies, waits for them, and re-layouts: 15 us -> 18.9 us
    all_to_all x0 -> x1, blocking collectives: none -> 99 us  [edit_chains(): lax.all_to_all(jnp.stack([base_x] * lax.axis_size(dev_axis)), dev_axis, s...]
    all_gather x1 -> x0, waiting for transfers between devices: 73.9 us -> none  [shards(): lax.all_gather(arrived, DEV, axis=0, tiled=True).reshape(-1, model_dim)]
    another operation x0 -> x2, local copies, waits for them, and re-layouts: none -> 11.1 us  [the longest x1 7.3 us: shards(): all_rows = process_desk_now(arrived).reshape(-1, model_dim)]
    reduce_scatter x2, waiting for transfers between devices: 91.8 us -> 84.5 us  [sum_by_axis(): total = lax.psum_scatter(total, axis, scatter_dimension=0, tiled=True)]
    reshape x2 -> x1, local copies, waits for them, and re-layouts: 7.23 us -> 0.02 us  [the longest x1 7.21 us: shards(): lax.all_gather(arrived, DEV, axis=0, tiled=True).reshape(-1, model_dim)]
  transfers between devices with their start and end apart: 6 -> 5, of which waited for: 6 -> 5; matrix products, arithmetic and copies ran while one was open for 0% -> 0% of each run, Pallas kernels for 0% -> 0%
where the time goes in v1:
time: 388 us; the launch traced here: 387 us
  blocking collectives  157 us (40%)
  waiting for transfers between devices  151 us (39%)
  starting transfers between devices  23 us (6%)
  matrix products  20.1 us (5%)
  local copies, waits for them, and re-layouts  18.9 us (5%)
  between operations  13.7 us (4%)
    all_to_all x1, blocking collectives, edit_chains(): lax.all_to_all(jnp.stack([base_x] * lax.axis_size(dev_axis)), dev_axis, s...  99 us
    reduce_scatter x2, waiting for transfers between devices, sum_by_axis(): total = lax.psum_scatter(total, axis, scatter_dimension=0, tiled=True)  84.5 us
    all_to_all x1, waiting for transfers between devices, sent_to_all(): lax.all_to_all(jnp.broadcast_to(shard[None], (peers, *shard.shape)), axis...  48.6 us
    all_gather x1, blocking collectives, side_by_side(): lax.all_gather(both, axis, axis=dim, tiled=True)  26 us
    all_to_all x1, blocking collectives, sent_to_all(): lax.all_to_all(jnp.broadcast_to(shard[None], (peers, *shard.shape)), axis...  18.2 us
    all_to_all x1, blocking collectives, shards(): lax.all_to_all(outgoing, 'grp', split_axis=0, concat_axis=0, tiled=True)  14.3 us
    all_to_all x1, starting transfers between devices, shards(): lax.all_to_all(summed.astype(jnp.bfloat16).reshape(experts, slot_cap, mod...  12.4 us
    dot_general x1, matrix products, shards(): jnp.dot(hidden, down_weight[0], preferred_element_type=jnp.float32)  9.1 us
  transfers between devices with their start and end apart: 5, of which 5 were waited for; matrix products, arithmetic and copies ran while one was open for 0% of the time, Pallas kernels for 0%

profile of v1, /device:TPU:1, one launch (start us, length us, event | category | flops | bytes accessed | tf_op | source)
XLA Modules:
  0.0 387.4 jit_solution(4845573770387338301)
XLA Ops:
  6.6 0.9 negate_bitcast_fusion
  7.4 0.6 reduce-window.6
  8.1 0.2 slice_reduce_fusion
  8.2 0.2 reduce-window.9
  8.5 0.2 slice_reduce_fusion.1
  8.7 0.9 copy.73
  9.7 0.8 fusion.55
  10.4 1.0 convolution_convert_fusion.2
  11.5 0.1 pad_maximum_fusion
  11.6 26.0 %all_gather.3 = bf16[16,2,8193]{2,1,0:T(2,128)(2,1)S(1)} all-gather(bf16[1,2,8193]{2,1,0:T(2,128)(2,1)S(1)} %pad_maximum_fusion), channel_id=1, replica_groups=mesh['grp'=16,'dev_0'=4,'dev_1'=8] {'grp'}, dimensions={0}, use_global_device_ids=true | all-gather | bytes 557124 | tf_op jit(solution)/shard_map/all_gather | solution.py:29
  37.6 0.7 slice.40
  38.3 0.1 copy.90
  38.8 0.4 reshape.244
  39.2 1.1 fusion.56
  40.3 0.6 fusion.15
  40.8 0.2 fusion.4
  41.1 0.6 fusion.3
  41.8 0.1 multiply_reduce_fusion
  42.0 18.2 %all_to_all.39 = f32[32,1,256]{2,1,0:T(1,128)S(1)} all-to-all(f32[32,1,256]{2,1,0:T(1,128)S(1)} %broadcast_in_dim.80), channel_id=1, replica_groups=mesh['grp'=16,'dev_0'=4,'dev_1'=8] {'dev_0','dev_1'}, dimensions={0} | all-to-all | bytes 65536 | tf_op jit(solution)/shard_map/all_to_all | solution.py:39
  60.3 0.1 multiply_convert_fusion
  60.4 0.1 copy.80
  60.5 1.6 broadcast_in_dim.81
  62.1 4.1 %all-to-all-start.1 = ((bf16[32,256,128]{1,2,0:T(8,128)(2,1)}), bf16[32,256,128]{1,2,0:T(8,128)(2,1)S(1)}, u32[]{:S(2)}, u32[]{:S(2)}) async-start(bf16[32,256,128]{1,2,0:T(8,128)(2,1)} %broadcast_in_dim.81), calls=%async_computation.1 | async-start | bytes 4194304 | tf_op jit(solution)/shard_map/all_to_all | solution.py:39
  66.5 0.2 select_reduce_fusion
  66.9 48.6 %all-to-all-done.1 = bf16[32,256,128]{1,2,0:T(8,128)(2,1)S(1)} async-done(((bf16[32,256,128]{1,2,0:T(8,128)(2,1)}), bf16[32,256,128]{1,2,0:T(8,128)(2,1)S(1)}, u32[]{:S(2)}, u32[]{:S(2)}) %all-to-all-start.1) | async-done | bytes 2097184 | tf_op jit(solution)/shard_map/all_to_all | solution.py:39
  115.5 1.5 convolution_convert_fusion.3
  117.0 0.1 copy.81
  117.1 0.7 reshape.258
  117.9 6.4 %all-to-all-start.2 = ((bf16[32,2,256]{2,1,0:T(2,128)(2,1)}), bf16[32,2,256]{2,1,0:T(2,128)(2,1)S(1)}, u32[]{:S(2)}, u32[]{:S(2)}) async-start(bf16[32,2,256]{2,1,0:T(2,128)(2,1)} %reshape.258), calls=%async_computation.2 | async-start | bytes 65536 | tf_op jit(solution)/shard_map/all_to_all | solution.py:165
  124.4 8.6 %all-to-all-done.2 = bf16[32,2,256]{2,1,0:T(2,128)(2,1)S(1)} async-done(((bf16[32,2,256]{2,1,0:T(2,128)(2,1)}), bf16[32,2,256]{2,1,0:T(2,128)(2,1)S(1)}, u32[]{:S(2)}, u32[]{:S(2)}) %all-to-all-start.2) | async-done | bytes 32800 | tf_op jit(solution)/shard_map/all_to_all | solution.py:165
  133.0 0.1 reshape.259
  133.2 0.1 reshape.251
  133.3 0.1 fusion.34
  133.5 0.2 convolution_convert_fusion.1
  133.7 0.1 reshape.247
  133.8 14.3 %all_to_all.40 = bf16[16,2,2048]{2,1,0:T(2,128)(2,1)S(1)} all-to-all(bf16[16,2,2048]{2,1,0:T(2,128)(2,1)S(1)} %reshape.247), channel_id=1, replica_groups=mesh['grp'=16,'dev_0'=4,'dev_1'=8] {'grp'}, dimensions={0} | all-to-all | bytes 262144 | tf_op jit(solution)/shard_map/all_to_all | solution.py:181
  148.1 3.8 stack.2
  151.9 99.0 %all_to_all.41 = bf16[32,16,2,2048]{3,2,1,0:T(2,128)(2,1)} all-to-all(bf16[32,16,2,2048]{3,2,1,0:T(2,128)(2,1)S(1)} %stack.2), channel_id=1, replica_groups=mesh['grp'=16,'dev_0'=4,'dev_1'=8] {'dev_0','dev_1'}, dimensions={0} | all-to-all | bytes 8388608 | tf_op jit(solution)/shard_map/all_to_all | solution.py:16
  250.9 7.3 %reshape_reshape.3 = bf16[1024,2048]{1,0:T(8,128)(2,1)} reshape(bf16[32,16,2,2048]{3,2,1,0:T(2,128)(2,1)} %all_to_all.41) | data formatting | bytes 8388608 | tf_op jit(solution)/shard_map/reshape;reshape | solution.py:182
  258.2 4.5 %fusion.8 = f32[1024,256]{1,0:T(8,128)} fusion(bf16[1024,2048]{1,0:T(8,128)(2,1)} %reshape_reshape.3, bf16[1,2048,256]{2,1,0:T(8,128)(2,1)S(1)} %copy-done.8), kind=kOutput, calls=%fused_computation.15 | convolution fusion | flops 1073741824 | bytes 6291456 | tf_op jit(solution)/shard_map/dot_general | solution.py:183
  262.7 9.1 %convolution_convert_fusion = bf16[1024,2048]{1,0:T(8,128)(2,1)} fusion(bf16[1024,2048]{1,0:T(8,128)(2,1)} %reshape_reshape.3, bf16[1,256,2048]{2,1,0:T(8,128)(2,1)S(1)} %copy-done, bf16[1,2048,256]{2,1,0:T(8,128)(2,1)} %param.30, f32[1024,256]{1,0:T(8,128)} %fusion.8), kind=kOutput, calls=%fused_computation | convolution fusion | flops 2151153664 | bytes 11534336 | tf_op jit(solution)/shard_map/dot_general | solution.py:186
  271.9 45.0 %reduce-scatter.3.cloned.1.call-done = bf16[256,2048]{1,0:T(8,128)(2,1)} async-done(((bf16[1024,2048]{1,0:T(8,128)(2,1)}), bf16[256,2048]{1,0:T(8,128)(2,1)}) %reduce-scatter.3.cloned.1.call-update) | async-done | bytes 1048592 | tf_op jit(solution)/shard_map/reduce_scatter | solution.py:62
  317.0 39.4 %reduce-scatter.5.cloned.1.call-done = bf16[32,2048]{1,0:T(8,128)(2,1)} async-done(((bf16[256,2048]{1,0:T(8,128)(2,1)}), bf16[32,2048]{1,0:T(8,128)(2,1)}) %reduce-scatter.5.cloned.1.call-update) | async-done | bytes 131088 | tf_op jit(solution)/shard_map/reduce_scatter | solution.py:62
  356.4 1.6 reshape.248
  358.1 12.4 %all-to-all-start.5 = ((bf16[16,2,2048]{2,1,0:T(2,128)(2,1)}), bf16[16,2,2048]{2,1,0:T(2,128)(2,1)S(1)}, u32[]{:S(2)}, u32[]{:S(2)}) async-start(bf16[16,2,2048]{2,1,0:T(2,128)(2,1)} %reshape.248), calls=%async_computation.7 | async-start | bytes 262144 | tf_op jit(solution)/shard_map/all_to_all | solution.py:187
  370.5 0.3 select_reduce_fusion.2
  370.9 8.8 %all-to-all-done.5 = bf16[16,2,2048]{2,1,0:T(2,128)(2,1)S(1)} async-done(((bf16[16,2,2048]{2,1,0:T(2,128)(2,1)}), bf16[16,2,2048]{2,1,0:T(2,128)(2,1)S(1)}, u32[]{:S(2)}, u32[]{:S(2)}) %all-to-all-start.5) | async-done | bytes 131104 | tf_op jit(solution)/shard_map/all_to_all | solution.py:187
  379.7 0.9 fusion
  (59 shorter events, 1.6 us)
Async XLA Ops:
  6.5 256.1 %copy-start = (bf16[1,256,2048]{2,1,0:T(8,128)(2,1)S(1)}, bf16[1,256,2048]{2,1,0:T(8,128)(2,1)}, u32[]{:S(2)}) copy-start(bf16[1,256,2048]{2,1,0:T(8,128)(2,1)} %param.31) | copy-start | bytes 3145732
  6.5 34.5 %copy-start.5 = (f32[256,2]{0,1:T(2,128)S(1)}, f32[256,2]{0,1:T(2,128)}, u32[]{:S(2)}) copy-start(f32[256,2]{0,1:T(2,128)} %param.18) | copy-start | bytes 6148
  6.5 34.3 %copy-start.2 = (bf16[256,128]{1,0:T(8,128)(2,1)S(1)}, bf16[256,128]{1,0:T(8,128)(2,1)}, u32[]{:S(2)}) copy-start(bf16[256,128]{1,0:T(8,128)(2,1)} %param.21) | copy-start | bytes 196612
  6.5 34.5 %copy-start.10 = (f32[2]{0:T(128)S(1)}, f32[2]{0:T(128)}, u32[]{:S(2)}) copy-start(f32[2]{0:T(128)} %param.22) | copy-start | bytes 28
  6.5 35.3 %copy-start.1 = (bf16[256,128]{1,0:T(8,128)(2,1)S(1)}, bf16[256,128]{1,0:T(8,128)(2,1)}, u32[]{:S(2)}) copy-start(bf16[256,128]{1,0:T(8,128)(2,1)} %param.17) | copy-start | bytes 196612
  6.5 53.7 %copy-start.7 = (f32[128]{0:T(128)S(1)}, f32[128]{0:T(128)}, u32[]{:S(2)}) copy-start(f32[128]{0:T(128)} %param.23) | copy-start | bytes 1540
  41.1 25.2 %copy-start.6 = (s32[8,2]{0,1:T(2,128)S(1)}, s32[8,2]{0,1:T(2,128)}, u32[]{:S(2)}) copy-start(s32[8,2]{0,1:T(2,128)} %param.28) | copy-start | bytes 196
  62.1 71.2 %copy-start.3 = (bf16[8,2048]{1,0:T(8,128)(2,1)S(1)}, bf16[8,2048]{1,0:T(8,128)(2,1)}, u32[]{:S(2)}) copy-start(bf16[8,2048]{1,0:T(8,128)(2,1)} %param.25) | copy-start | bytes 98308
  62.1 71.4 %copy-start.4 = (f32[2048]{0:T(1024)S(1)}, f32[2048]{0:T(1024)}, u32[]{:S(2)}) copy-start(f32[2048]{0:T(1024)} %param.26) | copy-start | bytes 24580
  62.1 53.4 %all-to-all-start.1 = ((bf16[32,256,128]{1,2,0:T(8,128)(2,1)}), bf16[32,256,128]{1,2,0:T(8,128)(2,1)S(1)}, u32[]{:S(2)}, u32[]{:S(2)}) async-start(bf16[32,256,128]{1,2,0:T(8,128)(2,1)} %broadcast_in_dim.81), calls=%async_computation.1 | async-start | bytes 4194304 | tf_op jit(solution)/shard_map/all_to_all | solution.py:39
  117.9 15.2 %all-to-all-start.2 = ((bf16[32,2,256]{2,1,0:T(2,128)(2,1)}), bf16[32,2,256]{2,1,0:T(2,128)(2,1)S(1)}, u32[]{:S(2)}, u32[]{:S(2)}) async-start(bf16[32,2,256]{2,1,0:T(2,128)(2,1)} %reshape.258), calls=%async_computation.2 | async-start | bytes 65536 | tf_op jit(solution)/shard_map/all_to_all | solution.py:165
  124.3 192.6 %reduce-scatter.3.cloned.1.call-start = ((), (), s32[]{:S(2)}) async-start(), calls=%async_computation.8 | async-start | bytes 5242880 | tf_op jit(solution)/shard_map/reduce_scatter | solution.py:62
  250.9 7.3 %copy-start.8 = (bf16[1,2048,256]{2,1,0:T(8,128)(2,1)S(1)}, bf16[1,2048,256]{2,1,0:T(8,128)(2,1)}, u32[]{:S(2)}) copy-start(bf16[1,2048,256]{2,1,0:T(8,128)(2,1)} %param.29) | copy-start | bytes 3145732
  271.8 98.7 %copy-start.9 = (f32[2048,16]{0,1:T(8,128)S(1)}, f32[2048,16]{0,1:T(8,128)}, u32[]{:S(2)}) copy-start(f32[2048,16]{0,1:T(8,128)} %param.27) | copy-start | bytes 393220
  271.8 84.6 %reduce-scatter.5.cloned.1.call-start = ((), (), s32[]{:S(2)}) async-start(), calls=%async_computation.9 | async-start | bytes 1179648 | tf_op jit(solution)/shard_map/reduce_scatter | solution.py:62
  358.1 21.6 %all-to-all-start.5 = ((bf16[16,2,2048]{2,1,0:T(2,128)(2,1)}), bf16[16,2,2048]{2,1,0:T(2,128)(2,1)S(1)}, u32[]{:S(2)}, u32[]{:S(2)}) async-start(bf16[16,2,2048]{2,1,0:T(2,128)(2,1)} %reshape.248), calls=%async_computation.7 | async-start | bytes 262144 | tf_op jit(solution)/shard_map/all_to_all | solution.py:187
Sparse Core Ops, SparseCore 0:
  271.9 44.9 reduce-scatter.2
  320.0 36.4 reduce-scatter.4
